TPU v7x, 32 devices: a whole 2x2x4 slice. The times are simulated.
32 devices in a mesh: groups: 2 (over y), tensor: 4 (over x, core), dp: 4 (over z).
Axes of the slice: x: 2, y: 2, z: 4, core: 2. Of those that a mesh axis runs over, the one named last changes fastest.
Arguments:
- tokens: bfloat16 [65536, 4096], P(('groups', 'dp'), 'tensor'), parts along dimension 0, may hold values from -6 to 6
- cotangent: bfloat16 [65536, 4096], P(('groups', 'dp'), 'tensor'), parts along dimension 0, may hold values from -6 to 6
- w_first: bfloat16 [16, 256, 256], P('tensor'), may hold values from -0.375 to 0.375
- w_second: bfloat16 [16, 256, 256], P('tensor'), may hold values from -0.375 to 0.375
Outputs:
- grad_tokens: bfloat16 [65536, 4096], P(('groups', 'dp'), 'tensor'), parts along dimension 0
- grad_first: float32 [32, 256, 256], P(('groups', 'tensor'), 'dp'), parts along dimension 0
- grad_second: float32 [32, 256, 256], P(('groups', 'tensor'), 'dp'), parts along dimension 0
There are 2 independent parts, one for each index of `groups`. A program takes and returns all parts, laid end to end along the dimension named above; an argument that names none is the same for every part. Nothing has to cross between parts.
All inputs are finite; a program needn't handle non-finite values.
Results may differ from a plain program's by a relative error of at most 0.0065.
Values may be sent and summed in bfloat16 or wider, within the bound.
No kernel may reach another device: no remote copies, remote signals or barrier semaphores. Data moves between devices by JAX's collectives and lax.ppermute only.
A program may use at most 192 MiB of HBM per device.

v0:
```python
import math
import jax
import jax.numpy as jnp
from jax import lax
from jax.sharding import PartitionSpec as P

NB = 16


def shards(tokens, cotangent, w_first, w_second):
    tok_rows = tokens.shape[0]
    blk_local = w_first.shape[0]
    blk_width = w_first.shape[1]
    sub_width = blk_width // NB
    dp_count = lax.axis_size("dp")
    grad_scale = 1.0 / math.sqrt(tok_rows * dp_count)
    inputs = tokens.reshape(tok_rows, blk_local, blk_width)
    upstream = cotangent.reshape(tok_rows, blk_local, blk_width)
    hidden = jnp.einsum("tbi,bij->bjt", inputs, w_first, preferred_element_type=jnp.float32).astype(
        jnp.bfloat16
    )
    hidden = hidden.reshape(blk_local, NB, sub_width, tok_rows)
    second_view = w_second.reshape(blk_local, sub_width, NB, blk_width)
    moved = lax.all_to_all(hidden, "tensor", split_axis=1, concat_axis=0, tiled=True)
    active = jnp.maximum(moved, jnp.zeros((), jnp.bfloat16))
    second_term = jnp.einsum("bcjt,tco->cjbo", active, upstream, preferred_element_type=jnp.float32)
    second_term = second_term.reshape(blk_local, blk_width, blk_width) * grad_scale
    backed = jnp.einsum("tco,cjbo->bcjt", upstream, second_view, preferred_element_type=jnp.float32)
    masked = jnp.where(moved > 0, backed, jnp.zeros((), jnp.float32)).astype(jnp.bfloat16)
    returned = lax.all_to_all(masked, "tensor", split_axis=0, concat_axis=1, tiled=True)
    returned = returned.reshape(blk_local, blk_width, tok_rows)
    first_term = (
        jnp.einsum("tbi,bjt->bij", inputs, returned, preferred_element_type=jnp.float32)
        * grad_scale
    )
    grad_tokens = jnp.einsum("bjt,bij->tbi", returned, w_first, preferred_element_type=jnp.float32)
    grad_tokens = grad_tokens.astype(jnp.bfloat16).reshape(tok_rows, blk_local * blk_width)
    grad_first, grad_second = (
        lax.psum_scatter(first_term, "dp", scatter_dimension=1, tiled=True),
        lax.psum_scatter(second_term, "dp", scatter_dimension=1, tiled=True),
    )
    return (grad_tokens, grad_first, grad_second)


def solution(mesh):
    return jax.shard_map(
        shards,
        mesh=mesh,
        in_specs=(
            P(("groups", "dp"), "tensor"),
            P(("groups", "dp"), "tensor"),
            P("tensor", None, None),
            P("tensor", None, None),
        ),
        out_specs=(
            P(("groups", "dp"), "tensor"),
            P(("groups", "tensor"), "dp", None),
            P(("groups", "tensor"), "dp", None),
        ),
        check_vma=False,
    )
```

profile of v0, /device:TPU:0, one launch (start us, length us, event | category | flops | bytes accessed | tf_op | source)
XLA Modules:
  0.0 638.0 jit_solution(12787721479795042683)
XLA Ops:
  7.2 1.0 copy-done
  8.2 20.5 %fusion.5 = bf16[4,256,8192]{2,1,0:T(8,128)(2,1)} fusion(bf16[4,256,256]{2,1,0:T(8,128)(2,1)S(1)} %copy-done, bf16[1024,4,8,256]{3,2,1,0:T(8,128)(2,1)} %bitcast.56), kind=kOutput, calls=%fused_computation.7 | convolution fusion | flops 4303355904 | bytes 34078720 | tf_op jit(solution)/shard_map/tbi,bij->bjt/dot_general | solution.py:19
  28.8 13.9 %copy.30 = bf16[4,16,16,8192]{3,2,0,1:T(8,128)(2,1)} copy(bf16[4,16,16,8192]{3,2,1,0:T(8,128)(2,1)} %bitcast.53) | data formatting | bytes 33554432 | tf_op jit(solution)/shard_map/reshape | solution.py:22
  42.6 7.0 %all-to-all-start = ((bf16[4,16,16,8192]{3,2,0,1:T(8,128)(2,1)}), bf16[4,16,16,8192]{3,2,0,1:T(8,128)(2,1)}, u32[]{:S(2)}, u32[]{:S(2)}) async-start(bf16[4,16,16,8192]{3,2,0,1:T(8,128)(2,1)} %copy.30), calls=%async_computation | async-start | bytes 33554432 | tf_op jit(solution)/shard_map/all_to_all | solution.py:24
  49.6 27.9 %reshape.39 = bf16[8192,4,256]{2,1,0:T(4,128)(2,1)} reshape(bf16[8192,1024]{1,0:T(8,128)(2,1)} %param.5) | data formatting | bytes 33554432 | tf_op jit(solution)/shard_map/reshape | solution.py:18
  77.5 155.8 %all-to-all-done = bf16[4,16,16,8192]{3,2,0,1:T(8,128)(2,1)} async-done(((bf16[4,16,16,8192]{3,2,0,1:T(8,128)(2,1)}), bf16[4,16,16,8192]{3,2,0,1:T(8,128)(2,1)}, u32[]{:S(2)}, u32[]{:S(2)}) %all-to-all-start) | async-done | bytes 16777248 | tf_op jit(solution)/shard_map/all_to_all | solution.py:24
  233.3 7.4 %broadcast_compare_fusion = pred[4,16,16,8192]{3,2,0,1:T(8,128)(4,1)S(1)} fusion(bf16[4,16,16,8192]{3,2,0,1:T(8,128)(2,1)} %all-to-all-done), kind=kLoop, calls=%fused_computation.15 | loop fusion | flops 8388608 | bytes 25165824 | tf_op jit(solution)/shard_map/gt | solution.py:29
  240.7 25.3 %copy.71 = pred[4,4,4,16,8192]{4,0,1,3,2:T(4,128)(4,1)} copy(pred[4,4,4,16,8192]{4,3,0,2,1:T(8,128)(4,1)S(1)} %bitcast.54) | data formatting | bytes 16777216 | tf_op jit(solution)/shard_map/gt | solution.py:29
  265.9 20.9 %gt.15 = pred[16,4,16,8192]{3,0,2,1:T(8,128)(4,1)} reshape(pred[4,4,4,16,8192]{4,1,0,3,2:T(4,128)(4,1)} %bitcast.55) | data formatting | bytes 16777216 | tf_op jit(solution)/shard_map/gt | solution.py:29
  286.8 24.9 %fusion = bf16[16,4,16,8192]{3,0,2,1:T(8,128)(2,1)} fusion(pred[16,4,16,8192]{3,0,2,1:T(8,128)(4,1)} %gt.15, bf16[4,16,16,256]{3,2,1,0:T(8,128)(2,1)S(1)} %bitcast.62, bf16[8192,4,256,1]{2,1,0,3:T(4,128)(2,1)} %bitcast.58), kind=kOutput, calls=%fused_computation.1 | convolution fusion | flops 4311744512 | bytes 42467328 | tf_op jit(solution)/shard_map/tco,cjbo->bcjt/dot_general | solution.py:28
  311.7 18.5 %copy.33 = bf16[16,4,16,8192]{3,2,1,0:T(8,128)(2,1)} copy(bf16[16,4,16,8192]{3,0,2,1:T(8,128)(2,1)} %fusion) | data formatting | bytes 33554432 | tf_op jit(solution)/shard_map/convert_element_type | solution.py:29
  330.1 7.1 %all-to-all-start.1 = ((bf16[16,4,16,8192]{3,2,1,0:T(8,128)(2,1)}), bf16[16,4,16,8192]{3,2,1,0:T(8,128)(2,1)}, u32[]{:S(2)}, u32[]{:S(2)}) async-start(bf16[16,4,16,8192]{3,2,1,0:T(8,128)(2,1)} %copy.33), calls=%async_computation.1 | async-start | bytes 33554432 | tf_op jit(solution)/shard_map/all_to_all | solution.py:30
  337.5 8.0 %broadcast_maximum_fusion = bf16[4,16,16,8192]{3,2,0,1:T(8,128)(2,1)S(1)} fusion(bf16[4,16,16,8192]{3,2,0,1:T(8,128)(2,1)} %all-to-all-done), kind=kLoop, calls=%fused_computation.14 | loop fusion | flops 8388608 | bytes 33554432 | tf_op jit(solution)/shard_map/max | solution.py:25
  345.4 6.6 %copy.37 = bf16[4,4,4,16,8192]{4,3,0,1,2:T(8,128)(2,1)} copy(bf16[4,4,4,16,8192]{4,3,0,2,1:T(8,128)(2,1)S(1)} %bitcast.51) | data formatting | bytes 33554432 | tf_op jit(solution)/shard_map/max | solution.py:25
  352.0 168.3 %all-to-all-done.1 = bf16[16,4,16,8192]{3,2,1,0:T(8,128)(2,1)} async-done(((bf16[16,4,16,8192]{3,2,1,0:T(8,128)(2,1)}), bf16[16,4,16,8192]{3,2,1,0:T(8,128)(2,1)}, u32[]{:S(2)}, u32[]{:S(2)}) %all-to-all-start.1) | async-done | bytes 16777248 | tf_op jit(solution)/shard_map/all_to_all | solution.py:30
  520.3 13.9 %copy.34 = bf16[4,4,4,16,8192]{4,3,2,0,1:T(8,128)(2,1)} copy(bf16[4,4,4,16,8192]{4,3,2,1,0:T(8,128)(2,1)} %bitcast.6) | data formatting | bytes 33554432 | tf_op jit(solution)/shard_map/all_to_all | solution.py:30
  534.2 12.9 %fusion.22 = f32[4,256,256]{1,2,0:T(8,128)S(1)} fusion(bf16[4,256,8192]{2,1,0:T(8,128)(2,1)} %bitcast.49, bf16[1024,4,8,256]{3,2,1,0:T(8,128)(2,1)} %bitcast.57), kind=kOutput, calls=%fused_computation.19 | convolution fusion | flops 4295229440 | bytes 34603008 | tf_op jit(solution)/shard_map/tbi,bjt->bij/dot_general | solution.py:33
  547.1 1.4 copy.36
  548.6 13.1 %fusion.16 = f32[4,16,16,256]{3,1,2,0:T(8,128)S(1)} fusion(bf16[16,4,16,8192]{3,2,0,1:T(8,128)(2,1)} %bitcast.60, bf16[8192,4,256,1]{2,1,0,3:T(4,128)(2,1)} %bitcast.59), kind=kOutput, calls=%fused_computation.17 | convolution fusion | flops 4295229440 | bytes 34603008 | tf_op jit(solution)/shard_map/bcjt,tco->cjbo/dot_general | solution.py:26
  561.7 1.6 copy.39
  564.6 13.9 %convolution_convert_fusion = bf16[4,8192,256]{1,2,0:T(8,128)(2,1)} fusion(bf16[4,256,256]{2,1,0:T(8,128)(2,1)S(1)} %copy-done, bf16[4,256,8192]{2,1,0:T(8,128)(2,1)} %bitcast.50), kind=kOutput, calls=%fused_computation.8 | convolution fusion | flops 4303355904 | bytes 34078720 | tf_op jit(solution)/shard_map/bjt,bij->tbi/dot_general | solution.py:36
  578.5 22.5 %copy.40 = bf16[8192,1024]{1,0:T(8,128)(2,1)} copy(bf16[8192,1024]{0,1:T(8,128)(2,1)} %bitcast.52) | data formatting | bytes 33554432
  601.7 1.0 constant_dynamic-slice_fusion
  603.4 27.8 %reduce-scatter.2.cloned.1.call-done = f32[4,64,256]{2,1,0:T(8,128)} async-done(((f32[4,256,256]{2,1,0:T(8,128)}), f32[4,64,256]{2,1,0:T(8,128)}) %reduce-scatter.2.cloned.1.call-update) | async-done | bytes 262160 | tf_op jit(solution)/shard_map/reduce_scatter | solution.py:40
  (12 shorter events, 2.3 us)
Async XLA Ops:
  7.2 1.0 copy-start
  42.6 190.6 %all-to-all-start = ((bf16[4,16,16,8192]{3,2,0,1:T(8,128)(2,1)}), bf16[4,16,16,8192]{3,2,0,1:T(8,128)(2,1)}, u32[]{:S(2)}, u32[]{:S(2)}) async-start(bf16[4,16,16,8192]{3,2,0,1:T(8,128)(2,1)} %copy.30), calls=%async_computation | async-start | bytes 33554432 | tf_op jit(solution)/shard_map/all_to_all | solution.py:24
  240.7 46.1 %copy-start.1 = (bf16[4,256,256]{2,1,0:T(8,128)(2,1)S(1)}, bf16[4,256,256]{2,1,0:T(8,128)(2,1)}, u32[]{:S(2)}) copy-start(bf16[4,256,256]{2,1,0:T(8,128)(2,1)} %param.7) | copy-start | bytes 1572868
  330.1 190.2 %all-to-all-start.1 = ((bf16[16,4,16,8192]{3,2,1,0:T(8,128)(2,1)}), bf16[16,4,16,8192]{3,2,1,0:T(8,128)(2,1)}, u32[]{:S(2)}, u32[]{:S(2)}) async-start(bf16[16,4,16,8192]{3,2,1,0:T(8,128)(2,1)} %copy.33), calls=%async_computation.1 | async-start | bytes 33554432 | tf_op jit(solution)/shard_map/all_to_all | solution.py:30
  337.2 264.4 %all-reduce.3.cloned.1.call-start = ((), (), s32[]{:S(2)}) async-start(), calls=%async_computation.4 | async-start | bytes 2097152
  548.5 82.6 %reduce-scatter.2.cloned.1.call-start = ((), (), s32[]{:S(2)}) async-start(), calls=%async_computation.3 | async-start | bytes 1310720 | tf_op jit(solution)/shard_map/reduce_scatter | solution.py:40
  548.6 14.8 %copy-start.2 = (u32[32]{0:T(128)S(1)}, u32[32]{0:T(128)}, u32[]{:S(2)}) copy-start(u32[32]{0:T(128)} %constant.8) | copy-start | bytes 388
Sparse Core Ops, SparseCore 0:
  548.6 52.9 all-reduce.2
  604.6 26.5 reduce-scatter.1
where the time goes:
time: 641 us; the launch traced here: 638 us
  waiting for transfers between devices  353 us (55%)
  local copies, waits for them, and re-layouts  156 us (24%)
  matrix products  85.4 us (13%)
  other arithmetic  15.3 us (2%)
  between operations  14.8 us (2%)
  starting transfers between devices  14.3 us (2%)
    all_to_all x1, waiting for transfers between devices, shards(): lax.all_to_all(masked, 'tensor', split_axis=0, concat_axis=1, tiled=True)  168 us
    all_to_all x1, waiting for transfers between devices, shards(): lax.all_to_all(hidden, 'tensor', split_axis=1, concat_axis=0, tiled=True)  156 us
    gt x2, local copies, waits for them, and re-layouts, shards(): moved > 0  46.1 us
    reshape x1, local copies, waits for them, and re-layouts, shards(): upstream = cotangent.reshape(tok_rows, blk_local, blk_width)  27.9 us
    reduce_scatter x1, waiting for transfers between devices, shards(): lax.psum_scatter(second_term, 'dp', scatter_dimension=1, tiled=True)  27.8 us
    unnamed x10, local copies, waits for them, and re-layouts  25.8 us
    dot_general x1, matrix products, shards(): jnp.einsum('tco,cjbo->bcjt', upstream, second_view, preferred_element_typ...  24.9 us
    dot_general x1, matrix products, shards(): jnp.einsum('tbi,bij->bjt', inputs, w_first, preferred_element_type=jnp.fl...  20.5 us
  transfers between devices with their start and end apart: 4, of which 4 were waited for; matrix products, arithmetic and copies ran while one was open for 15% of the time, Pallas kernels for 0%

commit v1 on v0

--- a/solution.py
+++ b/solution.py
@@ -21,7 +21,12 @@
     )
     hidden = hidden.reshape(blk_local, NB, sub_width, tok_rows)
     second_view = w_second.reshape(blk_local, sub_width, NB, blk_width)
-    moved = lax.all_to_all(hidden, "tensor", split_axis=1, concat_axis=0, tiled=True)
+    moved = jnp.concatenate(
+        lax.all_to_all(
+            jnp.stack(jnp.split(hidden, lax.axis_size("tensor"), axis=1)), "tensor", 0, 0
+        ),
+        axis=0,
+    )
     active = jnp.maximum(moved, jnp.zeros((), jnp.bfloat16))
     second_term = jnp.einsum("bcjt,tco->cjbo", active, upstream, preferred_element_type=jnp.float32)
     second_term = second_term.reshape(blk_local, blk_width, blk_width) * grad_scale

time: 641 us -> 605 us (0.944)
  local copies, waits for them, and re-layouts: 156 us -> 102 us
  other arithmetic: 15.3 us -> 25.5 us
  matrix products: 85.4 us -> 93.5 us
    gt x2 -> x0, local copies, waits for them, and re-layouts: 46.1 us -> none  [shards(): moved > 0]
    reshape x1 -> x0, local copies, waits for them, and re-layouts: 13.9 us -> none  [shards(): hidden = hidden.reshape(blk_local, NB, sub_width, tok_rows)]
    dot_general x1, matrix products: 24.9 us -> 33 us  [shards(): jnp.einsum('tco,cjbo->bcjt', upstream, second_view, preferred_element_typ...]
    another operation x0 -> x1, other arithmetic: none -> 7.03 us  [shards(): jnp.stack(jnp.split(hidden, lax.axis_size('tensor'), axis=1))]
    another operation x0 -> x1, local copies, waits for them, and re-layouts: none -> 6.49 us  [shards(): jnp.stack(jnp.split(hidden, lax.axis_size('tensor'), axis=1))]
  transfers between devices with their start and end apart: 4 -> 4, of which waited for: 4 -> 4; matrix products, arithmetic and copies ran while one was open for 15% -> 16% of each run, Pallas kernels for 0% -> 0%
where the time goes in v1:
time: 605 us; the launch traced here: 603 us
  waiting for transfers between devices  352 us (58%)
  local copies, waits for them, and re-layouts  102 us (17%)
  matrix products  93.5 us (15%)
  other arithmetic  25.5 us (4%)
  between operations  14.8 us (2%)
  starting transfers between devices  14.6 us (2%)
    all_to_all x1, waiting for transfers between devices, shards(): lax.all_to_all(masked, 'tensor', split_axis=0, concat_axis=1, tiled=True)  168 us
    all_to_all x1, waiting for transfers between devices, shards(): lax.all_to_all(jnp.stack(jnp.split(hidden, lax.axis_size('tensor'), axis=...  156 us
    dot_general x1, matrix products, shards(): jnp.einsum('tco,cjbo->bcjt', upstream, second_view, preferred_element_typ...  33 us
    reshape x1, local copies, waits for them, and re-layouts, shards(): upstream = cotangent.reshape(tok_rows, blk_local, blk_width)  27.9 us
    reduce_scatter x1, waiting for transfers between devices, shards(): lax.psum_scatter(second_term, 'dp', scatter_dimension=1, tiled=True)  27.8 us
    unnamed x10, local copies, waits for them, and re-layouts  25.8 us
    dot_general x1, matrix products, shards(): jnp.einsum('tbi,bij->bjt', inputs, w_first, preferred_element_type=jnp.fl...  20.5 us
    convert_element_type x1, local copies, waits for them, and re-layouts, shards(): jnp.where(moved > 0, backed, jnp.zeros((), jnp.float32))  18.5 us
  transfers between devices with their start and end apart: 4, of which 4 were waited for; matrix products, arithmetic and copies ran while one was open for 16% of the time, Pallas kernels for 0%

profile of v1, /device:TPU:0, one launch (start us, length us, event | category | flops | bytes accessed | tf_op | source)
XLA Modules:
  0.0 602.8 jit_solution(13479205193895212360)
XLA Ops:
  7.2 1.0 copy-done
  8.2 20.5 %fusion.5 = bf16[4,256,8192]{2,1,0:T(8,128)(2,1)} fusion(bf16[4,256,256]{2,1,0:T(8,128)(2,1)S(1)} %copy-done, bf16[1024,4,8,256]{3,2,1,0:T(8,128)(2,1)} %bitcast.53), kind=kOutput, calls=%fused_computation.7 | convolution fusion | flops 4303355904 | bytes 34078720 | tf_op jit(solution)/shard_map/tbi,bij->bjt/dot_general | solution.py:19
  28.8 6.5 %slice_bitcast_fusion.3 = (bf16[1,4,4,16,8192]{4,3,2,1,0:T(8,128)(2,1)S(1)}, bf16[1,4,4,16,8192]{4,3,2,1,0:T(8,128)(2,1)S(1)}, bf16[1,4,4,16,8192]{4,3,2,1,0:T(8,128)(2,1)S(1)}, bf16[1,4,4,16,8192]{4,3,2,1,0:T(8,128)(2,1)S(1)}) fusion(bf16[4,16,16,8192]{3,2,1,0:T(8,128)(2,1)} %bitcast.51), kind=kLoop, calls=%fused_computation.19 | loop fusion | bytes 33554432 | tf_op jit(solution)/shard_map/stack | solution.py:26
  35.3 7.0 %pad_maximum_fusion = bf16[4,4,4,16,8192]{4,3,2,1,0:T(8,128)(2,1)} fusion(bf16[1,4,4,16,8192]{4,3,2,1,0:T(8,128)(2,1)S(1)} %get-tuple-element.13, bf16[1,4,4,16,8192]{4,3,2,1,0:T(8,128)(2,1)S(1)} %get-tuple-element.14, bf16[1,4,4,16,8192]{4,3,2,1,0:T(8,128)(2,1)S(1)} %get-tuple-element.15, bf16[1,4,4,16,8192]{4,3,2,1,0:T(8,128)(2,1)S(1)} %get-tuple-element.12), kind=kLoop, calls=%fused_computation.6 | loop fusion | flops 25165824 | bytes 33554432 | tf_op jit(solution)/shard_map/stack | solution.py:26
  42.3 7.2 %all-to-all-start = ((bf16[4,4,4,16,8192]{4,3,2,1,0:T(8,128)(2,1)}), bf16[4,4,4,16,8192]{4,3,2,1,0:T(8,128)(2,1)}, u32[]{:S(2)}, u32[]{:S(2)}) async-start(bf16[4,4,4,16,8192]{4,3,2,1,0:T(8,128)(2,1)} %pad_maximum_fusion), calls=%async_computation | async-start | bytes 33554432 | tf_op jit(solution)/shard_map/all_to_all | solution.py:25
  49.4 27.9 %reshape.36 = bf16[8192,4,256]{2,1,0:T(4,128)(2,1)} reshape(bf16[8192,1024]{1,0:T(8,128)(2,1)} %param.5) | data formatting | bytes 33554432 | tf_op jit(solution)/shard_map/reshape | solution.py:18
  77.3 155.7 %all-to-all-done = bf16[4,4,4,16,8192]{4,3,2,1,0:T(8,128)(2,1)} async-done(((bf16[4,4,4,16,8192]{4,3,2,1,0:T(8,128)(2,1)}), bf16[4,4,4,16,8192]{4,3,2,1,0:T(8,128)(2,1)}, u32[]{:S(2)}, u32[]{:S(2)}) %all-to-all-start) | async-done | bytes 16777248 | tf_op jit(solution)/shard_map/all_to_all | solution.py:25
  233.1 10.4 %broadcast_compare_fusion = pred[4,4,4,16,8192]{4,3,2,1,0:T(8,128)(4,1)} fusion(bf16[4,4,4,16,8192]{4,3,2,1,0:T(8,128)(2,1)} %all-to-all-done), kind=kLoop, calls=%fused_computation.15 | loop fusion | flops 8388608 | bytes 25165824 | tf_op jit(solution)/shard_map/gt | solution.py:34
  243.5 33.0 %fusion = bf16[16,4,16,8192]{3,0,2,1:T(8,128)(2,1)} fusion(pred[16,4,16,8192]{3,2,1,0:T(8,128)(4,1)} %bitcast.58, bf16[4,16,16,256]{3,2,1,0:T(8,128)(2,1)S(1)} %bitcast.60, bf16[8192,4,256,1]{2,1,0,3:T(4,128)(2,1)} %bitcast.55), kind=kOutput, calls=%fused_computation.1 | convolution fusion | flops 4311744512 | bytes 42467328 | tf_op jit(solution)/shard_map/tco,cjbo->bcjt/dot_general | solution.py:33
  276.5 18.5 %copy.32 = bf16[16,4,16,8192]{3,2,1,0:T(8,128)(2,1)} copy(bf16[16,4,16,8192]{3,0,2,1:T(8,128)(2,1)} %fusion) | data formatting | bytes 33554432 | tf_op jit(solution)/shard_map/convert_element_type | solution.py:34
  295.0 7.1 %all-to-all-start.1 = ((bf16[16,4,16,8192]{3,2,1,0:T(8,128)(2,1)}), bf16[16,4,16,8192]{3,2,1,0:T(8,128)(2,1)}, u32[]{:S(2)}, u32[]{:S(2)}) async-start(bf16[16,4,16,8192]{3,2,1,0:T(8,128)(2,1)} %copy.32), calls=%async_computation.1 | async-start | bytes 33554432 | tf_op jit(solution)/shard_map/all_to_all | solution.py:35
  302.4 8.0 %broadcast_maximum_fusion = bf16[4,4,4,16,8192]{4,3,2,1,0:T(8,128)(2,1)S(1)} fusion(bf16[4,4,4,16,8192]{4,3,2,1,0:T(8,128)(2,1)} %all-to-all-done), kind=kLoop, calls=%fused_computation.14 | loop fusion | flops 8388608 | bytes 33554432 | tf_op jit(solution)/shard_map/max | solution.py:30
  310.4 6.5 %copy.36 = bf16[4,4,4,16,8192]{4,3,1,0,2:T(8,128)(2,1)} copy(bf16[4,4,4,16,8192]{4,3,2,1,0:T(8,128)(2,1)S(1)} %broadcast_maximum_fusion) | data formatting | bytes 33554432 | tf_op jit(solution)/shard_map/max | solution.py:30
  316.9 168.2 %all-to-all-done.1 = bf16[16,4,16,8192]{3,2,1,0:T(8,128)(2,1)} async-done(((bf16[16,4,16,8192]{3,2,1,0:T(8,128)(2,1)}), bf16[16,4,16,8192]{3,2,1,0:T(8,128)(2,1)}, u32[]{:S(2)}, u32[]{:S(2)}) %all-to-all-start.1) | async-done | bytes 16777248 | tf_op jit(solution)/shard_map/all_to_all | solution.py:35
  485.2 14.0 %copy.33 = bf16[4,4,4,16,8192]{4,3,2,0,1:T(8,128)(2,1)} copy(bf16[4,4,4,16,8192]{4,3,2,1,0:T(8,128)(2,1)} %bitcast.9) | data formatting | bytes 33554432 | tf_op jit(solution)/shard_map/all_to_all | solution.py:35
  499.2 12.9 %fusion.22 = f32[4,256,256]{1,2,0:T(8,128)S(1)} fusion(bf16[4,256,8192]{2,1,0:T(8,128)(2,1)} %bitcast.49, bf16[1024,4,8,256]{3,2,1,0:T(8,128)(2,1)} %bitcast.54), kind=kOutput, calls=%fused_computation.23 | convolution fusion | flops 4295229440 | bytes 34603008 | tf_op jit(solution)/shard_map/tbi,bjt->bij/dot_general | solution.py:38
  512.1 1.4 copy.35
  513.6 13.1 %fusion.16 = f32[4,16,16,256]{3,1,2,0:T(8,128)S(1)} fusion(bf16[16,4,16,8192]{3,2,0,1:T(8,128)(2,1)} %bitcast.57, bf16[8192,4,256,1]{2,1,0,3:T(4,128)(2,1)} %bitcast.56), kind=kOutput, calls=%fused_computation.21 | convolution fusion | flops 4295229440 | bytes 34603008 | tf_op jit(solution)/shard_map/bcjt,tco->cjbo/dot_general | solution.py:31
  526.7 1.6 copy.38
  529.6 13.9 %convolution_convert_fusion = bf16[4,8192,256]{1,2,0:T(8,128)(2,1)} fusion(bf16[4,256,256]{2,1,0:T(8,128)(2,1)S(1)} %copy-done, bf16[4,256,8192]{2,1,0:T(8,128)(2,1)} %bitcast.50), kind=kOutput, calls=%fused_computation.8 | convolution fusion | flops 4303355904 | bytes 34078720 | tf_op jit(solution)/shard_map/bjt,bij->tbi/dot_general | solution.py:41
  543.5 22.5 %copy.39 = bf16[8192,1024]{1,0:T(8,128)(2,1)} copy(bf16[8192,1024]{0,1:T(8,128)(2,1)} %bitcast.52) | data formatting | bytes 33554432
  566.5 1.0 constant_dynamic-slice_fusion
  567.4 0.8 copy.40
  568.2 27.8 %reduce-scatter.2.cloned.1.call-done = f32[4,64,256]{2,1,0:T(8,128)} async-done(((f32[4,256,256]{2,1,0:T(8,128)}), f32[4,64,256]{2,1,0:T(8,128)}) %reduce-scatter.2.cloned.1.call-update) | async-done | bytes 262160 | tf_op jit(solution)/shard_map/reduce_scatter | solution.py:45
  (11 shorter events, 1.4 us)
Async XLA Ops:
  7.2 1.0 copy-start
  42.3 190.8 %all-to-all-start = ((bf16[4,4,4,16,8192]{4,3,2,1,0:T(8,128)(2,1)}), bf16[4,4,4,16,8192]{4,3,2,1,0:T(8,128)(2,1)}, u32[]{:S(2)}, u32[]{:S(2)}) async-start(bf16[4,4,4,16,8192]{4,3,2,1,0:T(8,128)(2,1)} %pad_maximum_fusion), calls=%async_computation | async-start | bytes 33554432 | tf_op jit(solution)/shard_map/all_to_all | solution.py:25
  77.3 166.2 %copy-start.1 = (bf16[4,256,256]{2,1,0:T(8,128)(2,1)S(1)}, bf16[4,256,256]{2,1,0:T(8,128)(2,1)}, u32[]{:S(2)}) copy-start(bf16[4,256,256]{2,1,0:T(8,128)(2,1)} %param.7) | copy-start | bytes 1572868
  295.0 190.2 %all-to-all-start.1 = ((bf16[16,4,16,8192]{3,2,1,0:T(8,128)(2,1)}), bf16[16,4,16,8192]{3,2,1,0:T(8,128)(2,1)}, u32[]{:S(2)}, u32[]{:S(2)}) async-start(bf16[16,4,16,8192]{3,2,1,0:T(8,128)(2,1)} %copy.32), calls=%async_computation.1 | async-start | bytes 33554432 | tf_op jit(solution)/shard_map/all_to_all | solution.py:35
  302.1 264.3 %all-reduce.3.cloned.1.call-start = ((), (), s32[]{:S(2)}) async-start(), calls=%async_computation.4 | async-start | bytes 2097152
  513.5 82.5 %reduce-scatter.2.cloned.1.call-start = ((), (), s32[]{:S(2)}) async-start(), calls=%async_computation.3 | async-start | bytes 1310720 | tf_op jit(solution)/shard_map/reduce_scatter | solution.py:45
  513.5 14.8 %copy-start.2 = (u32[32]{0:T(128)S(1)}, u32[32]{0:T(128)}, u32[]{:S(2)}) copy-start(u32[32]{0:T(128)} %constant.8) | copy-start | bytes 388
Sparse Core Ops, SparseCore 0:
  513.6 52.7 all-reduce.2
  569.4 26.5 reduce-scatter.1
